TPU v7x, 32 devices: a whole 2x2x4 slice. The times are simulated.
32 devices in a mesh: row: 4 (over z), col: 8 (over y, x, core).
Axes of the slice: x: 2, y: 2, z: 4, core: 2. Of those that a mesh axis runs over, the one named last changes fastest.
Arguments:
- positions: float32 [3, 4, 8, 64], P(None, 'row', 'col'), may hold values from 0 to 32, as said below
- species: int32 [4, 8, 64], P('row', 'col'), may hold values from 0 to 3
- descriptors: float32 [128, 4, 8, 64], P(None, 'row', 'col'), may hold values from -6 to 6
- readout: float32 [4, 128], replicated, may hold values from -0.5 to 0.5
- hardness: float32 [4], replicated, may hold values from 1 to 4
- widths: float32 [4], replicated, may hold values from 0.5 to 1.5
Outputs:
- charges: float32 [4, 8, 64], P('row', 'col')
- forces: float32 [3, 4, 8, 64], P(None, 'row', 'col')
Inputs may be any that keep to these rules, and one draw needn't show every extreme that they name: `positions`: the atoms of brick (b, c) lie in [4 b, 4 b + 4) x [4 c, 4 c + 4) x [0, 4); no two atoms are closer than 0.4.
All inputs are finite; a program needn't handle non-finite values.
Results may differ from a plain program's by a relative error of at most 0.0003.
Values sent between devices are 32-bit elements; how exact they have to be, the bound alone decides.
No kernel may reach another device: no remote copies, remote signals or barrier semaphores. Data moves between devices by JAX's collectives and lax.ppermute only.
A program may use at most 64 MiB of HBM per device.

v0:
```python
import jax
import jax.numpy as jnp
from jax import lax
from jax.sharding import PartitionSpec as P

ITERS = 3
ROOT_PI = 1.7724538509055159
TWO_ROOT = 1.1283791670955126


def screened(row_geometry, col_geometry, self_pair):
    squared = jnp.zeros(self_pair.shape, row_geometry.dtype)
    for axis_id in range(3):
        separation = row_geometry[axis_id][:, None] - col_geometry[axis_id][None, :]
        squared = squared + separation * separation
    squared = jnp.where(self_pair, 1.0, squared)
    inverse = lax.rsqrt(squared)
    screening = lax.rsqrt(2.0 * (row_geometry[3][:, None] + col_geometry[3][None, :]))
    return jnp.where(self_pair, 0.0, lax.erf(screening * squared * inverse) * inverse)


def pulling(row_geometry, col_geometry, self_pair, col_charges):
    separations = []
    squared = jnp.zeros(self_pair.shape, row_geometry.dtype)
    for axis_id in range(3):
        separation = row_geometry[axis_id][:, None] - col_geometry[axis_id][None, :]
        separations.append(separation)
        squared = squared + separation * separation
    squared = jnp.where(self_pair, 1.0, squared)
    inverse = lax.rsqrt(squared)
    screening = lax.rsqrt(2.0 * (row_geometry[3][:, None] + col_geometry[3][None, :]))
    slope = (
        (
            lax.erf(screening * squared * inverse) * inverse
            - TWO_ROOT * screening * jnp.exp(-screening * screening * squared)
        )
        * inverse
        * inverse
    )
    slope = jnp.where(self_pair, 0.0, slope) * col_charges[None, :]
    return jnp.stack(
        [
            jnp.sum(slope * separations[0], 1),
            jnp.sum(slope * separations[1], 1),
            jnp.sum(slope * separations[2], 1),
        ]
    )


def apply_kernel(row_geometry, col_geometry, self_pair, vectors):
    kernel = screened(row_geometry, col_geometry, self_pair)
    return jnp.sum(kernel[None, :, :] * vectors[:, None, :], 2)


def shards(positions, species, descriptors, readout, hardness, widths):
    per_brick = species.shape[-1]
    row_at = lax.axis_index("row")
    col_at = lax.axis_index("col")
    kind_range = jnp.arange(hardness.shape[0], dtype=jnp.int32)
    onehot = (kind_range[:, None] == species.reshape(1, per_brick)).astype(jnp.float32)
    hard_atom = jnp.sum(onehot * hardness[:, None], 0)
    width_atom = jnp.sum(onehot * widths[:, None], 0)
    features = descriptors.reshape(descriptors.shape[0], per_brick)
    atom_weights = jnp.zeros(features.shape, jnp.float32)
    for kind in range(hardness.shape[0]):
        atom_weights = atom_weights + onehot[kind][None, :] * readout[kind][:, None]
    negativity = jnp.sum(features * atom_weights, 0)
    self_term = hard_atom + 1.0 / (width_atom * ROOT_PI)
    own_geometry = jnp.concatenate(
        [positions, (width_atom * width_atom).reshape(1, 1, 1, per_brick)], 0
    )
    row_geometry = lax.all_gather(own_geometry, "col", axis=2, tiled=True).reshape(4, -1)
    col_geometry = lax.all_gather(own_geometry, "row", axis=1, tiled=True).reshape(4, -1)
    row_total = row_geometry.shape[1]
    block_rows = 512
    block_count = row_total // block_rows

    def pair_mask(row_index, col_index):
        same_slot = (
            row_index[:, None] - col_at * per_brick == col_index[None, :] - row_at * per_brick
        )
        return same_slot & (row_index[:, None] // per_brick == col_at)

    def sweep(segment, block_fn, rows_out):
        columns = segment.shape[-1]
        col_index = jnp.arange(columns, dtype=jnp.int32)

        def one_block(block):
            first_row = block * block_rows
            row_part = lax.dynamic_slice_in_dim(row_geometry, first_row, block_rows, 1)
            row_index = first_row + jnp.arange(block_rows, dtype=jnp.int32)
            return block_fn(row_part, col_geometry, pair_mask(row_index, col_index), segment)

        blocks = lax.map(one_block, jnp.arange(block_count, dtype=jnp.int32))
        return jnp.moveaxis(blocks, 0, 1).reshape(rows_out, row_total)

    def squares(resid):
        return lax.psum(jnp.sum(resid * resid, 1), ("row", "col"))

    rhs = jnp.stack([-negativity, jnp.ones((per_brick,), jnp.float32)])
    solution = jnp.zeros_like(rhs)
    resid = rhs
    direction = rhs
    norm_now = squares(resid)
    for iteration in range(ITERS):
        partial_value = sweep(lax.all_gather(direction, "row", axis=1, tiled=True), apply_kernel, 2)
        whole = lax.psum(partial_value, "col")
        mine = lax.dynamic_slice_in_dim(whole, col_at * per_brick, per_brick, 1)
        image = mine + self_term[None, :] * direction
        curvature = lax.psum(jnp.sum(direction * image, 1), ("row", "col"))
        step_size = norm_now / curvature
        solution = solution + step_size[:, None] * direction
        if iteration + 1 < ITERS:
            resid = resid - step_size[:, None] * image
            norm_next = squares(resid)
            direction = resid + (norm_next / norm_now)[:, None] * direction
            norm_now = norm_next
    totals = lax.psum(jnp.sum(solution, 1), ("row", "col"))
    lagrange = totals[0] / totals[1]
    charges = solution[0] - lagrange * solution[1]
    field_sums = jnp.zeros((3, row_total), jnp.float32) + sweep(
        lax.all_gather(charges, "row", axis=0, tiled=True), pulling, 3
    )
    whole_pull = lax.psum(field_sums, "col")
    mine_pull = lax.dynamic_slice_in_dim(whole_pull, col_at * per_brick, per_brick, 1)
    forces = (charges[None, :] * mine_pull).reshape(3, 1, 1, per_brick)
    return (charges.reshape(1, 1, per_brick), forces)


def solution(mesh):
    in_specs = (
        P(None, "row", "col", None),
        P("row", "col", None),
        P(None, "row", "col", None),
        P(),
        P(),
        P(),
    )
    out_specs = (P("row", "col", None), P(None, "row", "col", None))
    return jax.shard_map(shards, mesh=mesh, in_specs=in_specs, out_specs=out_specs, check_vma=False)
```

profile of v0, /device:TPU:0, one launch (start us, length us, event | category | flops | bytes accessed | tf_op | source)
XLA Modules:
  0.0 359.4 jit_solution(654294700805835680)
XLA Ops:
  0.7 0.6 copy-done.1
  1.4 0.7 copy-done.4
  2.1 10.4 %all_gather.18 = f32[4,1,8,64]{3,0,1,2:T(4,128)S(1)} all-gather(f32[4,1,1,64]{3,0,1,2:T(4,128)S(1)} %pad_maximum_fusion.1), channel_id=1, replica_groups=mesh['row'=4,'col'=8] {'col'}, dimensions={2}, use_global_device_ids=true | all-gather | bytes 9216 | tf_op jit(solution)/shard_map/all_gather | solution.py:72
  12.8 12.1 %all_gather.19 = f32[4,4,1,64]{3,0,2,1:T(4,128)S(1)} all-gather(f32[4,1,1,64]{3,0,2,1:T(4,128)S(1)} %fusion.29), channel_id=1, replica_groups=mesh['row'=4,'col'=8] {'row'}, dimensions={1}, use_global_device_ids=true | all-gather | bytes 5120 | tf_op jit(solution)/shard_map/all_gather | solution.py:73
  25.3 0.5 fusion.12
  25.9 0.7 copy-done.2
  26.5 0.2 fusion.13
  26.7 9.7 %all-gather.1 = f32[4,64,2]{1,2,0:T(2,128)S(1)} all-gather(f32[1,64,2]{1,2,0:T(2,128)S(1)} %pad_bitcast_fusion), channel_id=1, replica_groups=mesh['row'=4,'col'=8] {'row'}, dimensions={0}, use_global_device_ids=true | all-gather | bytes 2560 | tf_op jit(solution)/shard_map/all_gather | solution.py:106
  36.5 0.2 multiply_reduce_fusion.2
  36.7 11.8 %psum.78 = f32[2,512]{1,0:T(2,128)S(1)} all-reduce(f32[2,512]{1,0:T(2,128)S(1)} %multiply_reduce_fusion.2), channel_id=1, replica_groups=mesh['row'=4,'col'=8] {'col'}, use_global_device_ids=true, to_apply=%region_5.6 | all-reduce | flops 1024 | bytes 8192 | tf_op jit(solution)/shard_map/psum | solution.py:107
  48.8 37.6 %all-reduce.2 = (f32[2]{0:T(128)S(1)}, f32[2]{0:T(128)S(1)}) all-reduce(f32[2]{0:T(128)S(1)} %get-tuple-element.86, f32[2]{0:T(128)S(1)} %get-tuple-element.85), channel_id=1, replica_groups=mesh['row'=4,'col'=8] {'row','col'}, use_global_device_ids=true, to_apply=%region_2.0 | all-reduce | flops 4 | bytes 32 | tf_op jit(solution)/shard_map/psum | solution.py:98
  86.4 0.2 multiply_reduce_fusion.6
  86.6 41.6 %psum.80 = f32[2]{0:T(128)S(1)} all-reduce(f32[2]{0:T(128)S(1)} %get-tuple-element.113), channel_id=1, replica_groups=mesh['row'=4,'col'=8] {'row','col'}, use_global_device_ids=true, to_apply=%region_10.11 | all-reduce | flops 2 | bytes 16 | tf_op jit(solution)/shard_map/psum | solution.py:98
  128.3 9.1 %all-gather.2 = f32[4,64,2]{1,2,0:T(2,128)S(1)} all-gather(f32[1,64,2]{1,2,0:T(2,128)S(1)} %fusion.28), channel_id=1, replica_groups=mesh['row'=4,'col'=8] {'row'}, dimensions={0}, use_global_device_ids=true | all-gather | bytes 2560 | tf_op jit(solution)/shard_map/all_gather | solution.py:106
  137.4 0.2 multiply_reduce_fusion.1
  137.7 11.8 %psum.81 = f32[2,512]{1,0:T(2,128)S(1)} all-reduce(f32[2,512]{1,0:T(2,128)S(1)} %multiply_reduce_fusion.1), channel_id=1, replica_groups=mesh['row'=4,'col'=8] {'col'}, use_global_device_ids=true, to_apply=%region_12.13 | all-reduce | flops 1024 | bytes 8192 | tf_op jit(solution)/shard_map/psum | solution.py:107
  149.7 38.5 %psum.82 = f32[2]{0:T(128)S(1)} all-reduce(f32[2]{0:T(128)S(1)} %multiply_reduce_fusion.5), channel_id=1, replica_groups=mesh['row'=4,'col'=8] {'row','col'}, use_global_device_ids=true, to_apply=%region_14.15 | all-reduce | flops 2 | bytes 16 | tf_op jit(solution)/shard_map/psum | solution.py:110
  188.2 0.2 multiply_reduce_fusion.4
  188.4 41.5 %psum.83 = f32[2]{0:T(128)S(1)} all-reduce(f32[2]{0:T(128)S(1)} %get-tuple-element.103), channel_id=1, replica_groups=mesh['row'=4,'col'=8] {'row','col'}, use_global_device_ids=true, to_apply=%region_16.17 | all-reduce | flops 2 | bytes 16 | tf_op jit(solution)/shard_map/psum | solution.py:98
  230.0 9.1 %all-gather.3 = f32[4,64,2]{1,2,0:T(2,128)S(1)} all-gather(f32[1,64,2]{1,2,0:T(2,128)S(1)} %bitcast.57), channel_id=1, replica_groups=mesh['row'=4,'col'=8] {'row'}, dimensions={0}, use_global_device_ids=true | all-gather | bytes 2560 | tf_op jit(solution)/shard_map/all_gather | solution.py:106
  239.2 0.2 multiply_reduce_fusion
  239.4 11.8 %psum.84 = f32[2,512]{1,0:T(2,128)S(1)} all-reduce(f32[2,512]{1,0:T(2,128)S(1)} %multiply_reduce_fusion), channel_id=1, replica_groups=mesh['row'=4,'col'=8] {'col'}, use_global_device_ids=true, to_apply=%region_18.19 | all-reduce | flops 1024 | bytes 8192 | tf_op jit(solution)/shard_map/psum | solution.py:107
  251.4 38.5 %psum.85 = f32[2]{0:T(128)S(1)} all-reduce(f32[2]{0:T(128)S(1)} %multiply_reduce_fusion.3), channel_id=1, replica_groups=mesh['row'=4,'col'=8] {'row','col'}, use_global_device_ids=true, to_apply=%region_20.21 | all-reduce | flops 2 | bytes 16 | tf_op jit(solution)/shard_map/psum | solution.py:110
  289.9 0.2 fusion.25
  290.1 41.5 %psum.86 = f32[2]{0:T(128)S(1)} all-reduce(f32[2]{0:T(128)S(1)} %get-tuple-element.101), channel_id=1, replica_groups=mesh['row'=4,'col'=8] {'row','col'}, use_global_device_ids=true, to_apply=%region_22.23 | all-reduce | flops 2 | bytes 16 | tf_op jit(solution)/shard_map/psum | solution.py:118
  331.7 0.6 fusion.27
  333.6 0.6 copy-done.7
  334.2 0.6 dynamic-slice
  335.6 9.9 %all-reduce.1 = f32[256]{0:T(256)S(1)} all-reduce(f32[256]{0:T(256)S(1)} %get-tuple-element.99), channel_id=2, replica_groups=mesh['row'=4,'col'=8] {'row'}, use_global_device_ids=true, to_apply=%add.1 | all-reduce | flops 256 | bytes 2048
  345.5 1.2 fusion.3
  346.7 12.0 %psum.87 = f32[3,512]{1,0:T(4,128)S(1)} all-reduce(f32[3,512]{1,0:T(4,128)S(1)} %pad_maximum_fusion), channel_id=1, replica_groups=mesh['row'=4,'col'=8] {'col'}, use_global_device_ids=true, to_apply=%region_26.27 | all-reduce | flops 1536 | bytes 12288 | tf_op jit(solution)/shard_map/psum | solution.py:124
  358.8 0.6 reshape.327
  (55 shorter events, 2.1 us)
Async XLA Ops:
  0.6 0.7 copy-start.1
  0.6 0.7 copy-start.6
  0.7 0.7 copy-start.5
  1.4 0.7 copy-start.4
  25.3 1.2 copy-start
  25.8 0.7 copy-start.2
  333.6 0.7 copy-start.7
  335.6 23.2 %copy-start.3 = (f32[1,64]{1,0:T(1,128)}, f32[1,64]{1,0:T(1,128)S(1)}, u32[]{:S(2)}) copy-start(f32[1,64]{1,0:T(1,128)S(1)} %get-tuple-element.100) | copy-start | bytes 772
where the time goes:
time: 361 us; the launch traced here: 359 us
  blocking collectives  347 us (96%)
  local copies, waits for them, and re-layouts  5.38 us (1%)
  other arithmetic  4.18 us (1%)
    psum x3, blocking collectives, squares(): return lax.psum(jnp.sum(resid * resid, 1), ('row', 'col'))  121 us
    psum x2, blocking collectives, shards(): curvature = lax.psum(jnp.sum(direction * image, 1), ('row', 'col'))  77.1 us
    psum x1, blocking collectives, shards(): totals = lax.psum(jnp.sum(solution, 1), ('row', 'col'))  41.5 us
    psum x3, blocking collectives, shards(): whole = lax.psum(partial_value, 'col')  35.4 us
    all_gather x3, blocking collectives, shards(): lax.all_gather(direction, 'row', axis=1, tiled=True)  27.9 us
    all_gather x1, blocking collectives, shards(): lax.all_gather(own_geometry, 'row', axis=1, tiled=True).reshape(4, -1)  12.1 us
    psum x1, blocking collectives, shards(): whole_pull = lax.psum(field_sums, 'col')  12 us
    all_gather x1, blocking collectives, shards(): lax.all_gather(own_geometry, 'col', axis=2, tiled=True).reshape(4, -1)  10.4 us

commit v1 on v0

--- a/solution.py
+++ b/solution.py
@@ -115,7 +115,7 @@
             norm_next = squares(resid)
             direction = resid + (norm_next / norm_now)[:, None] * direction
             norm_now = norm_next
-    totals = lax.psum(jnp.sum(solution, 1), ("row", "col"))
+    totals = lax.psum(lax.psum(jnp.sum(solution, 1), "col"), "row")
     lagrange = totals[0] / totals[1]
     charges = solution[0] - lagrange * solution[1]
     field_sums = jnp.zeros((3, row_total), jnp.float32) + sweep(

time: 361 us -> 341 us (0.945)
  blocking collectives: 347 us -> 327 us
    psum x1 -> x2, blocking collectives: 41.5 us -> 22.6 us  [shards(): totals = lax.psum(lax.psum(jnp.sum(solution, 1), 'col'), 'row')]
where the time goes in v1:
time: 341 us; the launch traced here: 339 us
  blocking collectives  327 us (96%)
  local copies, waits for them, and re-layouts  5.38 us (2%)
  other arithmetic  4.18 us (1%)
    psum x3, blocking collectives, squares(): return lax.psum(jnp.sum(resid * resid, 1), ('row', 'col'))  121 us
    psum x2, blocking collectives, shards(): curvature = lax.psum(jnp.sum(direction * image, 1), ('row', 'col'))  77.1 us
    psum x3, blocking collectives, shards(): whole = lax.psum(partial_value, 'col')  35.4 us
    all_gather x3, blocking collectives, shards(): lax.all_gather(direction, 'row', axis=1, tiled=True)  27.9 us
    psum x2, blocking collectives, shards(): totals = lax.psum(lax.psum(jnp.sum(solution, 1), 'col'), 'row')  22.6 us
    all_gather x1, blocking collectives, shards(): lax.all_gather(own_geometry, 'row', axis=1, tiled=True).reshape(4, -1)  12.1 us
    psum x1, blocking collectives, shards(): whole_pull = lax.psum(field_sums, 'col')  12 us
    all_gather x1, blocking collectives, shards(): lax.all_gather(own_geometry, 'col', axis=2, tiled=True).reshape(4, -1)  10.4 us

profile of v1, /device:TPU:0, one launch (start us, length us, event | category | flops | bytes accessed | tf_op | source)
XLA Modules:
  0.0 339.4 jit_solution(16048692008540789038)
XLA Ops:
  0.7 0.6 copy-done.1
  1.4 0.7 copy-done.4
  2.1 10.4 %all_gather.18 = f32[4,1,8,64]{3,0,1,2:T(4,128)S(1)} all-gather(f32[4,1,1,64]{3,0,1,2:T(4,128)S(1)} %pad_maximum_fusion.1), channel_id=1, replica_groups=mesh['row'=4,'col'=8] {'col'}, dimensions={2}, use_global_device_ids=true | all-gather | bytes 9216 | tf_op jit(solution)/shard_map/all_gather | solution.py:72
  12.8 12.1 %all_gather.19 = f32[4,4,1,64]{3,0,2,1:T(4,128)S(1)} all-gather(f32[4,1,1,64]{3,0,2,1:T(4,128)S(1)} %fusion.29), channel_id=1, replica_groups=mesh['row'=4,'col'=8] {'row'}, dimensions={1}, use_global_device_ids=true | all-gather | bytes 5120 | tf_op jit(solution)/shard_map/all_gather | solution.py:73
  25.3 0.5 fusion.12
  25.9 0.7 copy-done.2
  26.5 0.2 fusion.13
  26.7 9.7 %all-gather.1 = f32[4,64,2]{1,2,0:T(2,128)S(1)} all-gather(f32[1,64,2]{1,2,0:T(2,128)S(1)} %pad_bitcast_fusion), channel_id=1, replica_groups=mesh['row'=4,'col'=8] {'row'}, dimensions={0}, use_global_device_ids=true | all-gather | bytes 2560 | tf_op jit(solution)/shard_map/all_gather | solution.py:106
  36.5 0.2 multiply_reduce_fusion.2
  36.7 11.8 %psum.85 = f32[2,512]{1,0:T(2,128)S(1)} all-reduce(f32[2,512]{1,0:T(2,128)S(1)} %multiply_reduce_fusion.2), channel_id=1, replica_groups=mesh['row'=4,'col'=8] {'col'}, use_global_device_ids=true, to_apply=%region_5.6 | all-reduce | flops 1024 | bytes 8192 | tf_op jit(solution)/shard_map/psum | solution.py:107
  48.8 37.6 %all-reduce.2 = (f32[2]{0:T(128)S(1)}, f32[2]{0:T(128)S(1)}) all-reduce(f32[2]{0:T(128)S(1)} %get-tuple-element.86, f32[2]{0:T(128)S(1)} %get-tuple-element.85), channel_id=1, replica_groups=mesh['row'=4,'col'=8] {'row','col'}, use_global_device_ids=true, to_apply=%region_2.0 | all-reduce | flops 4 | bytes 32 | tf_op jit(solution)/shard_map/psum | solution.py:98
  86.4 0.2 multiply_reduce_fusion.6
  86.6 41.6 %psum.87 = f32[2]{0:T(128)S(1)} all-reduce(f32[2]{0:T(128)S(1)} %get-tuple-element.113), channel_id=1, replica_groups=mesh['row'=4,'col'=8] {'row','col'}, use_global_device_ids=true, to_apply=%region_10.11 | all-reduce | flops 2 | bytes 16 | tf_op jit(solution)/shard_map/psum | solution.py:98
  128.3 9.1 %all-gather.2 = f32[4,64,2]{1,2,0:T(2,128)S(1)} all-gather(f32[1,64,2]{1,2,0:T(2,128)S(1)} %fusion.28), channel_id=1, replica_groups=mesh['row'=4,'col'=8] {'row'}, dimensions={0}, use_global_device_ids=true | all-gather | bytes 2560 | tf_op jit(solution)/shard_map/all_gather | solution.py:106
  137.4 0.2 multiply_reduce_fusion.1
  137.7 11.8 %psum.88 = f32[2,512]{1,0:T(2,128)S(1)} all-reduce(f32[2,512]{1,0:T(2,128)S(1)} %multiply_reduce_fusion.1), channel_id=1, replica_groups=mesh['row'=4,'col'=8] {'col'}, use_global_device_ids=true, to_apply=%region_12.13 | all-reduce | flops 1024 | bytes 8192 | tf_op jit(solution)/shard_map/psum | solution.py:107
  149.7 38.5 %psum.89 = f32[2]{0:T(128)S(1)} all-reduce(f32[2]{0:T(128)S(1)} %multiply_reduce_fusion.5), channel_id=1, replica_groups=mesh['row'=4,'col'=8] {'row','col'}, use_global_device_ids=true, to_apply=%region_14.15 | all-reduce | flops 2 | bytes 16 | tf_op jit(solution)/shard_map/psum | solution.py:110
  188.2 0.2 multiply_reduce_fusion.4
  188.4 41.5 %psum.90 = f32[2]{0:T(128)S(1)} all-reduce(f32[2]{0:T(128)S(1)} %get-tuple-element.103), channel_id=1, replica_groups=mesh['row'=4,'col'=8] {'row','col'}, use_global_device_ids=true, to_apply=%region_16.17 | all-reduce | flops 2 | bytes 16 | tf_op jit(solution)/shard_map/psum | solution.py:98
  230.0 9.1 %all-gather.3 = f32[4,64,2]{1,2,0:T(2,128)S(1)} all-gather(f32[1,64,2]{1,2,0:T(2,128)S(1)} %bitcast.57), channel_id=1, replica_groups=mesh['row'=4,'col'=8] {'row'}, dimensions={0}, use_global_device_ids=true | all-gather | bytes 2560 | tf_op jit(solution)/shard_map/all_gather | solution.py:106
  239.2 0.2 multiply_reduce_fusion
  239.4 11.8 %psum.91 = f32[2,512]{1,0:T(2,128)S(1)} all-reduce(f32[2,512]{1,0:T(2,128)S(1)} %multiply_reduce_fusion), channel_id=1, replica_groups=mesh['row'=4,'col'=8] {'col'}, use_global_device_ids=true, to_apply=%region_18.19 | all-reduce | flops 1024 | bytes 8192 | tf_op jit(solution)/shard_map/psum | solution.py:107
  251.4 38.5 %psum.92 = f32[2]{0:T(128)S(1)} all-reduce(f32[2]{0:T(128)S(1)} %multiply_reduce_fusion.3), channel_id=1, replica_groups=mesh['row'=4,'col'=8] {'row','col'}, use_global_device_ids=true, to_apply=%region_20.21 | all-reduce | flops 2 | bytes 16 | tf_op jit(solution)/shard_map/psum | solution.py:110
  290.1 12.7 %psum.93 = f32[2]{0:T(128)S(1)} all-reduce(f32[2]{0:T(128)S(1)} %get-tuple-element.101), channel_id=1, replica_groups=mesh['row'=4,'col'=8] {'col'}, use_global_device_ids=true, to_apply=%region_22.23 | all-reduce | flops 2 | bytes 16 | tf_op jit(solution)/shard_map/psum | solution.py:118
  302.8 9.9 %psum.94 = f32[2]{0:T(128)S(1)} all-reduce(f32[2]{0:T(128)S(1)} %psum.93), channel_id=1, replica_groups=mesh['row'=4,'col'=8] {'row'}, use_global_device_ids=true, to_apply=%region_23.24 | all-reduce | flops 2 | bytes 16 | tf_op jit(solution)/shard_map/psum | solution.py:118
  312.7 0.6 fusion.27
  314.7 0.6 copy-done.7
  315.3 0.6 dynamic-slice
  316.7 8.8 %all-reduce.1 = f32[256]{0:T(256)S(1)} all-reduce(f32[256]{0:T(256)S(1)} %get-tuple-element.99), channel_id=2, replica_groups=mesh['row'=4,'col'=8] {'row'}, use_global_device_ids=true, to_apply=%add.1 | all-reduce | flops 256 | bytes 2048
  325.5 1.2 fusion.3
  326.7 12.0 %psum.95 = f32[3,512]{1,0:T(4,128)S(1)} all-reduce(f32[3,512]{1,0:T(4,128)S(1)} %pad_maximum_fusion), channel_id=1, replica_groups=mesh['row'=4,'col'=8] {'col'}, use_global_device_ids=true, to_apply=%region_27.28 | all-reduce | flops 1536 | bytes 12288 | tf_op jit(solution)/shard_map/psum | solution.py:124
  338.8 0.6 reshape.327
  (56 shorter events, 2.3 us)
Async XLA Ops:
  0.6 0.7 copy-start.1
  0.6 0.7 copy-start.6
  0.7 0.7 copy-start.5
  1.4 0.7 copy-start.4
  25.3 1.2 copy-start
  25.8 0.7 copy-start.2
  314.7 0.7 copy-start.7
  316.7 22.1 %copy-start.3 = (f32[1,64]{1,0:T(1,128)}, f32[1,64]{1,0:T(1,128)S(1)}, u32[]{:S(2)}) copy-start(f32[1,64]{1,0:T(1,128)S(1)} %get-tuple-element.100) | copy-start | bytes 772
